TPU v7x, 32 devices: a whole 2x2x4 slice. The times are simulated.
32 devices in a mesh: region: 2 (over y), mod: 4 (over z), obs: 4 (over x, core).
Axes of the slice: x: 2, y: 2, z: 4, core: 2. Of those that a mesh axis runs over, the one named last changes fastest.
Arguments:
- model_days: float32 [16384, 128], P(('region', 'mod')), parts along dimension 0, may hold values from -48 to 48
- obs_days: float32 [16384, 128], P(('region', 'obs', 'mod')), parts along dimension 0, may hold values from -48 to 48
Outputs:
- mapped: float32 [16384, 128], P(('region', 'mod', 'obs')), parts along dimension 0
- row_potential: float32 [16384], P(('region', 'mod')), parts along dimension 0
- col_potential: float32 [16384], P(('region', 'obs')), parts along dimension 0
There are 2 independent parts, one for each index of `region`. A program takes and returns all parts, laid end to end along the dimension named above; each array names one. Nothing has to cross between parts.
All inputs are finite; a program needn't handle non-finite values.
Results may differ from a plain program's by a relative error of at most 0.0003.
Values sent between devices are 32-bit elements; how exact they have to be, the bound alone decides.
No kernel may reach another device: no remote copies, remote signals or barrier semaphores. Data moves between devices by JAX's collectives and lax.ppermute only.
A program may use at most 64 MiB of HBM per device.

v0:
```python
import math
import jax
import jax.numpy as jnp
from jax import lax
from jax.sharding import PartitionSpec as P

ITERS = 2
entropy_scale = 0.02


def pair_cost(block_rows, block_square, columns):
    column_square = jnp.sum(columns * columns, axis=1)
    cross = lax.dot_general(
        block_rows,
        columns,
        (((1,), (1,)), ((), ())),
        precision=lax.Precision.HIGHEST,
        preferred_element_type=jnp.float32,
    )
    return (block_square[:, None] + column_square[None, :] - 2.0 * cross) / block_rows.shape[1]


def across_obs(peaks, totals):
    highest = lax.pmax(peaks, "obs")
    summed = lax.psum(totals * jnp.exp(peaks - highest), "obs")
    return highest + jnp.log(summed)


def across_mod(peaks, totals):
    highest = lax.pmax(peaks, "mod")
    summed = lax.psum(totals * jnp.exp(peaks - highest), "mod")
    return highest + jnp.log(summed)


def on_device(model_days, obs_days):
    row_square = jnp.sum(model_days * model_days, axis=1)
    row_count = model_days.shape[0]
    col_count = obs_days.shape[0] * lax.axis_size("mod")
    log_obs = math.log(col_count * lax.axis_size("obs"))
    log_model = math.log(row_count * lax.axis_size("mod"))
    gathered = lax.all_gather(obs_days, "mod", axis=0, tiled=True)
    cost_tile = pair_cost(model_days, row_square, gathered)

    def row_stats(col_potential):
        scores = (col_potential[None, :] - cost_tile) / entropy_scale
        peaks = jnp.max(scores, axis=1)
        return (peaks, jnp.sum(jnp.exp(scores - peaks[:, None]), axis=1))

    col_potential = jnp.zeros((col_count,), jnp.float32)
    for iteration in range(ITERS):
        peaks, totals = row_stats(col_potential)
        row_potential = -entropy_scale * (across_obs(peaks, totals) - log_obs)
        col_scores = (row_potential[:, None] - cost_tile) / entropy_scale
        col_peaks = jnp.max(col_scores, axis=0)
        peaks = col_peaks
        totals = jnp.sum(jnp.exp(col_scores - col_peaks[None, :]), axis=0)
        col_potential = -entropy_scale * (across_mod(peaks, totals) - log_model)
    peaks, totals = row_stats(col_potential)
    final_lse = across_obs(peaks, totals)
    row_potential = -entropy_scale * (final_lse - log_obs)
    weights = jnp.exp((col_potential[None, :] - cost_tile) / entropy_scale - final_lse[:, None])
    partial_map = jnp.dot(
        weights, gathered, precision=lax.Precision.HIGHEST, preferred_element_type=jnp.float32
    )
    summed_map = lax.psum(partial_map, "obs")
    share = row_count // lax.axis_size("obs")
    mapped = lax.dynamic_slice_in_dim(summed_map, lax.axis_index("obs") * share, share, 0)
    return (mapped, row_potential, col_potential)


def solution(mesh):
    in_specs = (P(("region", "mod"), None), P(("region", "obs", "mod"), None))
    out_specs = (P(("region", "mod", "obs"), None), P(("region", "mod")), P(("region", "obs")))
    return jax.shard_map(
        on_device, mesh=mesh, in_specs=in_specs, out_specs=out_specs, check_vma=False
    )
```

profile of v0, /device:TPU:0, one launch (start us, length us, event | category | flops | bytes accessed | tf_op | source)
XLA Modules:
  0.0 285.6 jit_solution(2504910936190339218)
XLA Ops:
  9.5 30.8 %all-gather.2.cloned.1.call-done = f32[2048,128]{1,0:T(8,128)} async-done(((f32[512,128]{1,0:T(8,128)}), f32[2048,128]{1,0:T(8,128)}) %all-gather.2.cloned.1.call-update) | async-done | bytes 1048592 | tf_op jit(solution)/shard_map/all_gather | solution.py:41
  41.9 20.6 %fusion.3 = (f32[2048]{0:T(1024)S(1)}, f32[2048,2048]{0,1:T(8,128)}) fusion(f32[2048,128]{1,0:T(8,128)} %param.2, f32[2048,128]{1,0:T(8,128)} %all-gather.2.cloned.1.call-done, f32[2048]{0:T(1024)S(1)} %multiply_reduce_fusion, f32[2048]{0:T(1024)S(1)} %multiply_reduce_fusion.1), kind=kOutput, calls=%fused_computation.14 | convolution fusion | flops 6471809024 | bytes 18898944 | tf_op jit(solution)/shard_map/dot_general | solution.py:13
  62.5 6.2 %pmax.35 = f32[2048]{0:T(1024)S(1)} all-reduce(f32[2048]{0:T(1024)S(1)} %get-tuple-element.5), channel_id=1, replica_groups=mesh['region'=2,'mod'=4,'obs'=4] {'obs'}, use_global_device_ids=true, to_apply=%region_3.0 | all-reduce | flops 2048 | bytes 16384 | tf_op jit(solution)/shard_map/pmax | solution.py:24
  68.6 9.1 %exponential_reduce_fusion.4 = f32[2048]{0:T(1024)S(1)} fusion(f32[2048,2048]{0,1:T(8,128)} %get-tuple-element.6, f32[2048]{0:T(1024)S(1)} %get-tuple-element.5), kind=kLoop, calls=%fused_computation.11 | loop fusion | flops 16775168 | bytes 16793600 | tf_op jit(solution)/shard_map/reduce_sum | solution.py:47
  77.7 6.4 %psum.42 = f32[2048]{0:T(1024)S(1)} all-reduce(f32[2048]{0:T(1024)S(1)} %exponential_multiply_fusion.4), channel_id=1, replica_groups=mesh['region'=2,'mod'=4,'obs'=4] {'obs'}, use_global_device_ids=true, to_apply=%region_5.0 | all-reduce | flops 2048 | bytes 16384 | tf_op jit(solution)/shard_map/psum | solution.py:25
  84.2 7.5 %fusion.4 = f32[2048]{0:T(1024)S(1)} fusion(f32[2048,2048]{0,1:T(8,128)} %get-tuple-element.6, f32[2048]{0:T(1024)S(1)} %add_multiply_fusion.4), kind=kLoop, calls=%fused_computation.15 | loop fusion | flops 12580864 | bytes 16793600 | tf_op jit(solution)/shard_map/reduce_max | solution.py:54
  91.7 8.0 %exponential_reduce_fusion.3 = f32[2048]{0:T(1024)S(1)} fusion(f32[2048,2048]{0,1:T(8,128)} %get-tuple-element.6, f32[2048]{0:T(1024)S(1)} %fusion.4, f32[2048]{0:T(1024)S(1)} %add_multiply_fusion.4), kind=kLoop, calls=%fused_computation.9 | loop fusion | flops 16775168 | bytes 16801792 | tf_op jit(solution)/shard_map/reduce_sum | solution.py:56
  99.7 11.0 %pmax.36 = f32[2048]{0:T(1024)S(1)} all-reduce(f32[2048]{0:T(1024)S(1)} %fusion.4), channel_id=1, replica_groups=mesh['region'=2,'mod'=4,'obs'=4] {'mod'}, use_global_device_ids=true, to_apply=%region_7.0 | all-reduce | flops 2048 | bytes 16384 | tf_op jit(solution)/shard_map/pmax | solution.py:30
  110.7 8.5 %psum.43 = f32[2048]{0:T(1024)S(1)} all-reduce(f32[2048]{0:T(1024)S(1)} %exponential_multiply_fusion.3), channel_id=1, replica_groups=mesh['region'=2,'mod'=4,'obs'=4] {'mod'}, use_global_device_ids=true, to_apply=%region_9.0 | all-reduce | flops 2048 | bytes 16384 | tf_op jit(solution)/shard_map/psum | solution.py:31
  119.2 7.5 %fusion.5 = f32[2048]{0:T(1024)S(1)} fusion(f32[2048,2048]{0,1:T(8,128)} %get-tuple-element.6, f32[2048]{0:T(1024)S(1)} %add_multiply_fusion.3), kind=kLoop, calls=%fused_computation.16 | loop fusion | flops 12580864 | bytes 16793600 | tf_op jit(solution)/shard_map/reduce_max | solution.py:46
  126.7 8.0 %exponential_reduce_fusion.2 = f32[2048]{0:T(1024)S(1)} fusion(f32[2048,2048]{0,1:T(8,128)} %get-tuple-element.6, f32[2048]{0:T(1024)S(1)} %fusion.5, f32[2048]{0:T(1024)S(1)} %add_multiply_fusion.3), kind=kLoop, calls=%fused_computation.7 | loop fusion | flops 16775168 | bytes 16801792 | tf_op jit(solution)/shard_map/reduce_sum | solution.py:47
  134.7 5.8 %pmax.37 = f32[2048]{0:T(1024)S(1)} all-reduce(f32[2048]{0:T(1024)S(1)} %fusion.5), channel_id=1, replica_groups=mesh['region'=2,'mod'=4,'obs'=4] {'obs'}, use_global_device_ids=true, to_apply=%region_11.0 | all-reduce | flops 2048 | bytes 16384 | tf_op jit(solution)/shard_map/pmax | solution.py:24
  140.5 6.3 %psum.44 = f32[2048]{0:T(1024)S(1)} all-reduce(f32[2048]{0:T(1024)S(1)} %exponential_multiply_fusion.2), channel_id=1, replica_groups=mesh['region'=2,'mod'=4,'obs'=4] {'obs'}, use_global_device_ids=true, to_apply=%region_13.0 | all-reduce | flops 2048 | bytes 16384 | tf_op jit(solution)/shard_map/psum | solution.py:25
  146.8 7.5 %fusion.6 = f32[2048]{0:T(1024)S(1)} fusion(f32[2048,2048]{0,1:T(8,128)} %get-tuple-element.6, f32[2048]{0:T(1024)S(1)} %add_multiply_fusion.2), kind=kLoop, calls=%fused_computation.17 | loop fusion | flops 12580864 | bytes 16793600 | tf_op jit(solution)/shard_map/reduce_max | solution.py:54
  154.4 8.0 %exponential_reduce_fusion.1 = f32[2048]{0:T(1024)S(1)} fusion(f32[2048,2048]{0,1:T(8,128)} %get-tuple-element.6, f32[2048]{0:T(1024)S(1)} %fusion.6, f32[2048]{0:T(1024)S(1)} %add_multiply_fusion.2), kind=kLoop, calls=%fused_computation.5 | loop fusion | flops 16775168 | bytes 16801792 | tf_op jit(solution)/shard_map/reduce_sum | solution.py:56
  162.3 10.2 %pmax.38 = f32[2048]{0:T(1024)S(1)} all-reduce(f32[2048]{0:T(1024)S(1)} %fusion.6), channel_id=1, replica_groups=mesh['region'=2,'mod'=4,'obs'=4] {'mod'}, use_global_device_ids=true, to_apply=%region_15.0 | all-reduce | flops 2048 | bytes 16384 | tf_op jit(solution)/shard_map/pmax | solution.py:30
  172.6 9.0 %psum.45 = f32[2048]{0:T(1024)S(1)} all-reduce(f32[2048]{0:T(1024)S(1)} %exponential_multiply_fusion.1), channel_id=1, replica_groups=mesh['region'=2,'mod'=4,'obs'=4] {'mod'}, use_global_device_ids=true, to_apply=%region_17.0 | all-reduce | flops 2048 | bytes 16384 | tf_op jit(solution)/shard_map/psum | solution.py:31
  181.7 7.6 %fusion.7 = f32[2048]{0:T(1024)S(1)} fusion(f32[2048,2048]{0,1:T(8,128)} %get-tuple-element.6, f32[2048]{0:T(1024)S(1)} %add_multiply_fusion.1), kind=kLoop, calls=%fused_computation.18 | loop fusion | flops 12580864 | bytes 16793600 | tf_op jit(solution)/shard_map/reduce_max | solution.py:46
  189.2 8.0 %exponential_reduce_fusion = f32[2048]{0:T(1024)S(1)} fusion(f32[2048,2048]{0,1:T(8,128)} %get-tuple-element.6, f32[2048]{0:T(1024)S(1)} %fusion.7, f32[2048]{0:T(1024)S(1)} %add_multiply_fusion.1), kind=kLoop, calls=%fused_computation.3 | loop fusion | flops 16775168 | bytes 16801792 | tf_op jit(solution)/shard_map/reduce_sum | solution.py:47
  197.2 5.8 %pmax.39 = f32[2048]{0:T(1024)S(1)} all-reduce(f32[2048]{0:T(1024)S(1)} %fusion.7), channel_id=1, replica_groups=mesh['region'=2,'mod'=4,'obs'=4] {'obs'}, use_global_device_ids=true, to_apply=%region_19.0 | all-reduce | flops 2048 | bytes 16384 | tf_op jit(solution)/shard_map/pmax | solution.py:24
  203.0 6.9 %psum.46 = f32[2048]{0:T(1024)S(1)} all-reduce(f32[2048]{0:T(1024)S(1)} %exponential_multiply_fusion), channel_id=1, replica_groups=mesh['region'=2,'mod'=4,'obs'=4] {'obs'}, use_global_device_ids=true, to_apply=%region_21.0 | all-reduce | flops 2048 | bytes 16384 | tf_op jit(solution)/shard_map/psum | solution.py:25
  210.5 31.6 %fusion = f32[2048,128]{1,0:T(8,128)} fusion(f32[2048,128]{1,0:T(8,128)S(1)} %copy-done, f32[2048,2048]{0,1:T(8,128)} %get-tuple-element.6, f32[2048]{0:T(1024)S(1)} %get-tuple-element.4, f32[2048]{0:T(1024)S(1)} %add_multiply_fusion.1), kind=kOutput, calls=%fused_computation | convolution fusion | flops 6455033856 | bytes 18890752 | tf_op jit(solution)/shard_map/dot_general | solution.py:62
  242.1 34.9 %all-reduce.2.cloned.1.call-done = f32[2048,128]{1,0:T(8,128)} async-done(((f32[2048,128]{1,0:T(8,128)}), f32[2048,128]{1,0:T(8,128)}) %all-reduce.2.cloned.1.call-update) | async-done | bytes 1048592 | tf_op jit(solution)/shard_map/psum | solution.py:65
  277.0 1.7 constant_dynamic-slice_fusion
  (20 shorter events, 4.6 us)
Async XLA Ops:
  7.2 33.1 %all-gather.2.cloned.1.call-start = ((), (), s32[]{:S(2)}) async-start(), calls=%async_computation | async-start | bytes 1310720 | tf_op jit(solution)/shard_map/all_gather | solution.py:41
  7.9 269.1 %all-reduce.2.cloned.1.call-start = ((), (), s32[]{:S(2)}) async-start(), calls=%async_computation.1 | async-start | bytes 2097152 | tf_op jit(solution)/shard_map/psum | solution.py:65
  181.7 28.9 %copy-start.1 = (f32[2048]{0:T(1024)}, f32[2048]{0:T(1024)S(1)}, u32[]{:S(2)}) copy-start(f32[2048]{0:T(1024)S(1)} %add_multiply_fusion.1) | copy-start | bytes 24580
  181.7 28.8 %copy-start = (f32[2048,128]{1,0:T(8,128)S(1)}, f32[2048,128]{1,0:T(8,128)}, u32[]{:S(2)}) copy-start(f32[2048,128]{1,0:T(8,128)} %all-gather.2.cloned.1.call-done) | copy-start | bytes 3145732
Sparse Core Ops, SparseCore 0:
  9.5 30.6 all-gather.1
  242.2 34.7 all-reduce.1
where the time goes:
time: 286 us
  blocking collectives  76.1 us (27%)
  other arithmetic  74.9 us (26%)
  waiting for transfers between devices  66.4 us (23%)
  matrix products  52.2 us (18%)
  between operations  14.2 us (5%)
    psum x1, waiting for transfers between devices, on_device(): summed_map = lax.psum(partial_map, 'obs')  34.9 us
    dot_general x1, matrix products, on_device(): jnp.dot(weights, gathered, precision=lax.Precision.HIGHEST, preferred_ele...  31.6 us
    all_gather x1, waiting for transfers between devices, on_device(): gathered = lax.all_gather(obs_days, 'mod', axis=0, tiled=True)  30.8 us
    reduce_sum x3, other arithmetic, row_stats(): return (peaks, jnp.sum(jnp.exp(scores - peaks[:, None]), axis=1))  25 us
    pmax x2, blocking collectives, across_mod(): highest = lax.pmax(peaks, 'mod')  21.2 us
    dot_general x1, matrix products, pair_cost(): lax.dot_general(block_rows, columns, (((1,), (1,)), ((), ())), precision=...  20.6 us
    psum x3, blocking collectives, across_obs(): summed = lax.psum(totals * jnp.exp(peaks - highest), 'obs')  19.7 us
    pmax x3, blocking collectives, across_obs(): highest = lax.pmax(peaks, 'obs')  17.7 us
  transfers between devices with their start and end apart: 2, of which 2 were waited for; matrix products, arithmetic and copies ran while one was open for 1% of the time, Pallas kernels for 0%

commit v1 on v0

--- a/solution.py
+++ b/solution.py
@@ -6,6 +6,28 @@
 
 ITERS = 2
 entropy_scale = 0.02
+
+
+def joined_along(blocks, dim):
+    blocks = jnp.moveaxis(blocks, 0, dim)
+    lengths = blocks.shape
+    return blocks.reshape(*lengths[:dim], lengths[dim] * lengths[dim + 1], *lengths[dim + 2 :])
+
+
+def gather_around(x, axis, dim):
+    count = lax.axis_size(axis)
+    pairs = [(i, (i + 1) % count) for i in range(count)]
+    back = [(b, a) for a, b in pairs]
+    lower, upper = ([], [])
+    for turn in range(count - 1):
+        if turn % 2 == 0:
+            lower.append(lax.ppermute(lower[-1] if lower else x, axis, pairs))
+        else:
+            upper.append(lax.ppermute(upper[-1] if upper else x, axis, back))
+    pieces = jnp.stack([*lower[::-1], x, *upper])
+    shift = lax.axis_index(axis) - len(lower)
+    pieces = pieces[(jnp.arange(count) - shift) % count]
+    return joined_along(pieces, dim)
 
 
 def pair_cost(block_rows, block_square, columns):
@@ -38,7 +60,7 @@
     col_count = obs_days.shape[0] * lax.axis_size("mod")
     log_obs = math.log(col_count * lax.axis_size("obs"))
     log_model = math.log(row_count * lax.axis_size("mod"))
-    gathered = lax.all_gather(obs_days, "mod", axis=0, tiled=True)
+    gathered = gather_around(obs_days, "mod", 0)
     cost_tile = pair_cost(model_days, row_square, gathered)
 
     def row_stats(col_potential):

time: 286 us -> 275 us (0.962)
  waiting for transfers between devices: 66.4 us -> 51.5 us
  starting transfers between devices: 0.08 us -> 5.24 us
    all_gather x1 -> x0, waiting for transfers between devices: 30.8 us -> none  [on_device(): gathered = lax.all_gather(obs_days, 'mod', axis=0, tiled=True)]
    ppermute x0 -> x3, waiting for transfers between devices: none -> 16.1 us  [the longest x2 13.3 us: gather_around(): lower.append(lax.ppermute(lower[-1] if lower else x, axis, pairs))]
    ppermute x0 -> x3, starting transfers between devices: none -> 5.2 us  [the longest x2 3.11 us: gather_around(): lower.append(lax.ppermute(lower[-1] if lower else x, axis, pairs))]
  transfers between devices with their start and end apart: 2 -> 4, of which waited for: 2 -> 4; matrix products, arithmetic and copies ran while one was open for 1% -> 1% of each run, Pallas kernels for 0% -> 0%
where the time goes in v1:
time: 275 us
  blocking collectives  75.6 us (27%)
  other arithmetic  74.6 us (27%)
  waiting for transfers between devices  51.5 us (19%)
  matrix products  51 us (19%)
  between operations  14.2 us (5%)
  starting transfers between devices  5.24 us (2%)
    psum x1, waiting for transfers between devices, on_device(): summed_map = lax.psum(partial_map, 'obs')  35.3 us
    dot_general x1, matrix products, on_device(): jnp.dot(weights, gathered, precision=lax.Precision.HIGHEST, preferred_ele...  31.5 us
    reduce_sum x3, other arithmetic, row_stats(): return (peaks, jnp.sum(jnp.exp(scores - peaks[:, None]), axis=1))  25 us
    pmax x2, blocking collectives, across_mod(): highest = lax.pmax(peaks, 'mod')  20.6 us
    psum x3, blocking collectives, across_obs(): summed = lax.psum(totals * jnp.exp(peaks - highest), 'obs')  20 us
    dot_general x1, matrix products, pair_cost(): lax.dot_general(block_rows, columns, (((1,), (1,)), ((), ())), precision=...  19.6 us
    psum x2, blocking collectives, across_mod(): summed = lax.psum(totals * jnp.exp(peaks - highest), 'mod')  17.5 us
    pmax x3, blocking collectives, across_obs(): highest = lax.pmax(peaks, 'obs')  17.5 us
  transfers between devices with their start and end apart: 4, of which 4 were waited for; matrix products, arithmetic and copies ran while one was open for 1% of the time, Pallas kernels for 0%

profile of v1, /device:TPU:0, one launch (start us, length us, event | category | flops | bytes accessed | tf_op | source)
XLA Modules:
  0.0 274.5 jit_solution(16848903617358490956)
XLA Ops:
  12.4 7.3 %collective-permute-done = f32[512,128]{1,0:T(8,128)S(1)} collective-permute-done((f32[512,128]{1,0:T(8,128)}, f32[512,128]{1,0:T(8,128)S(1)}, u32[]{:S(2)}, u32[]{:S(2)}) %collective-permute-start) | collective-permute-done | bytes 262176 | tf_op jit(solution)/shard_map/ppermute | solution.py:24
  24.1 6.0 %collective-permute-done.1 = f32[512,128]{1,0:T(8,128)S(1)} collective-permute-done((f32[512,128]{1,0:T(8,128)S(1)}, f32[512,128]{1,0:T(8,128)S(1)}, u32[]{:S(2)}, u32[]{:S(2)}) %collective-permute-start.1) | collective-permute-done | bytes 262176 | tf_op jit(solution)/shard_map/ppermute | solution.py:24
  32.1 19.6 %fusion.4 = (f32[2048]{0:T(1024)S(1)}, f32[2048,2048]{0,1:T(8,128)}) fusion(f32[2048,128]{1,0:T(8,128)S(1)} %bitcast.16, f32[2048,128]{1,0:T(8,128)} %param.2, f32[2048]{0:T(1024)S(1)} %bitcast.23, f32[2048]{0:T(1024)S(1)} %multiply_reduce_fusion.1), kind=kOutput, calls=%fused_computation.16 | convolution fusion | flops 6471809024 | bytes 18898944 | tf_op jit(solution)/shard_map/dot_general | solution.py:35
  51.7 5.7 %pmax.35 = f32[2048]{0:T(1024)S(1)} all-reduce(f32[2048]{0:T(1024)S(1)} %get-tuple-element.5), channel_id=1, replica_groups=mesh['region'=2,'mod'=4,'obs'=4] {'obs'}, use_global_device_ids=true, to_apply=%region_3.4 | all-reduce | flops 2048 | bytes 16384 | tf_op jit(solution)/shard_map/pmax | solution.py:46
  57.5 9.1 %exponential_reduce_fusion.4 = f32[2048]{0:T(1024)S(1)} fusion(f32[2048,2048]{0,1:T(8,128)} %get-tuple-element.6, f32[2048]{0:T(1024)S(1)} %get-tuple-element.5), kind=kLoop, calls=%fused_computation.14 | loop fusion | flops 16775168 | bytes 16793600 | tf_op jit(solution)/shard_map/reduce_sum | solution.py:69
  66.5 6.9 %psum.42 = f32[2048]{0:T(1024)S(1)} all-reduce(f32[2048]{0:T(1024)S(1)} %exponential_multiply_fusion.4), channel_id=1, replica_groups=mesh['region'=2,'mod'=4,'obs'=4] {'obs'}, use_global_device_ids=true, to_apply=%region_5.6 | all-reduce | flops 2048 | bytes 16384 | tf_op jit(solution)/shard_map/psum | solution.py:47
  73.4 7.5 %fusion.5 = f32[2048]{0:T(1024)S(1)} fusion(f32[2048,2048]{0,1:T(8,128)} %get-tuple-element.6, f32[2048]{0:T(1024)S(1)} %add_multiply_fusion.4), kind=kLoop, calls=%fused_computation.17 | loop fusion | flops 12580864 | bytes 16793600 | tf_op jit(solution)/shard_map/reduce_max | solution.py:76
  81.0 8.0 %exponential_reduce_fusion.3 = f32[2048]{0:T(1024)S(1)} fusion(f32[2048,2048]{0,1:T(8,128)} %get-tuple-element.6, f32[2048]{0:T(1024)S(1)} %fusion.5, f32[2048]{0:T(1024)S(1)} %add_multiply_fusion.4), kind=kLoop, calls=%fused_computation.12 | loop fusion | flops 16775168 | bytes 16801792 | tf_op jit(solution)/shard_map/reduce_sum | solution.py:78
  89.0 10.3 %pmax.36 = f32[2048]{0:T(1024)S(1)} all-reduce(f32[2048]{0:T(1024)S(1)} %fusion.5), channel_id=1, replica_groups=mesh['region'=2,'mod'=4,'obs'=4] {'mod'}, use_global_device_ids=true, to_apply=%region_7.8 | all-reduce | flops 2048 | bytes 16384 | tf_op jit(solution)/shard_map/pmax | solution.py:52
  99.2 8.8 %psum.43 = f32[2048]{0:T(1024)S(1)} all-reduce(f32[2048]{0:T(1024)S(1)} %exponential_multiply_fusion.3), channel_id=1, replica_groups=mesh['region'=2,'mod'=4,'obs'=4] {'mod'}, use_global_device_ids=true, to_apply=%region_9.10 | all-reduce | flops 2048 | bytes 16384 | tf_op jit(solution)/shard_map/psum | solution.py:53
  108.1 7.5 %fusion.6 = f32[2048]{0:T(1024)S(1)} fusion(f32[2048,2048]{0,1:T(8,128)} %get-tuple-element.6, f32[2048]{0:T(1024)S(1)} %add_multiply_fusion.3), kind=kLoop, calls=%fused_computation.18 | loop fusion | flops 12580864 | bytes 16793600 | tf_op jit(solution)/shard_map/reduce_max | solution.py:68
  115.5 8.0 %exponential_reduce_fusion.2 = f32[2048]{0:T(1024)S(1)} fusion(f32[2048,2048]{0,1:T(8,128)} %get-tuple-element.6, f32[2048]{0:T(1024)S(1)} %fusion.6, f32[2048]{0:T(1024)S(1)} %add_multiply_fusion.3), kind=kLoop, calls=%fused_computation.10 | loop fusion | flops 16775168 | bytes 16801792 | tf_op jit(solution)/shard_map/reduce_sum | solution.py:69
  123.5 5.8 %pmax.37 = f32[2048]{0:T(1024)S(1)} all-reduce(f32[2048]{0:T(1024)S(1)} %fusion.6), channel_id=1, replica_groups=mesh['region'=2,'mod'=4,'obs'=4] {'obs'}, use_global_device_ids=true, to_apply=%region_11.12 | all-reduce | flops 2048 | bytes 16384 | tf_op jit(solution)/shard_map/pmax | solution.py:46
  129.3 6.5 %psum.44 = f32[2048]{0:T(1024)S(1)} all-reduce(f32[2048]{0:T(1024)S(1)} %exponential_multiply_fusion.2), channel_id=1, replica_groups=mesh['region'=2,'mod'=4,'obs'=4] {'obs'}, use_global_device_ids=true, to_apply=%region_13.14 | all-reduce | flops 2048 | bytes 16384 | tf_op jit(solution)/shard_map/psum | solution.py:47
  135.8 7.5 %fusion.7 = f32[2048]{0:T(1024)S(1)} fusion(f32[2048,2048]{0,1:T(8,128)} %get-tuple-element.6, f32[2048]{0:T(1024)S(1)} %add_multiply_fusion.2), kind=kLoop, calls=%fused_computation.19 | loop fusion | flops 12580864 | bytes 16793600 | tf_op jit(solution)/shard_map/reduce_max | solution.py:76
  143.4 8.0 %exponential_reduce_fusion.1 = f32[2048]{0:T(1024)S(1)} fusion(f32[2048,2048]{0,1:T(8,128)} %get-tuple-element.6, f32[2048]{0:T(1024)S(1)} %fusion.7, f32[2048]{0:T(1024)S(1)} %add_multiply_fusion.2), kind=kLoop, calls=%fused_computation.8 | loop fusion | flops 16775168 | bytes 16801792 | tf_op jit(solution)/shard_map/reduce_sum | solution.py:78
  151.4 10.3 %pmax.38 = f32[2048]{0:T(1024)S(1)} all-reduce(f32[2048]{0:T(1024)S(1)} %fusion.7), channel_id=1, replica_groups=mesh['region'=2,'mod'=4,'obs'=4] {'mod'}, use_global_device_ids=true, to_apply=%region_15.16 | all-reduce | flops 2048 | bytes 16384 | tf_op jit(solution)/shard_map/pmax | solution.py:52
  161.7 8.7 %psum.45 = f32[2048]{0:T(1024)S(1)} all-reduce(f32[2048]{0:T(1024)S(1)} %exponential_multiply_fusion.1), channel_id=1, replica_groups=mesh['region'=2,'mod'=4,'obs'=4] {'mod'}, use_global_device_ids=true, to_apply=%region_17.18 | all-reduce | flops 2048 | bytes 16384 | tf_op jit(solution)/shard_map/psum | solution.py:53
  170.5 7.5 %fusion.8 = f32[2048]{0:T(1024)S(1)} fusion(f32[2048,2048]{0,1:T(8,128)} %get-tuple-element.6, f32[2048]{0:T(1024)S(1)} %add_multiply_fusion.1), kind=kLoop, calls=%fused_computation.20 | loop fusion | flops 12580864 | bytes 16793600 | tf_op jit(solution)/shard_map/reduce_max | solution.py:68
  177.9 6.0 %pmax.39 = f32[2048]{0:T(1024)S(1)} all-reduce(f32[2048]{0:T(1024)S(1)} %fusion.8), channel_id=1, replica_groups=mesh['region'=2,'mod'=4,'obs'=4] {'obs'}, use_global_device_ids=true, to_apply=%region_19.20 | all-reduce | flops 2048 | bytes 16384 | tf_op jit(solution)/shard_map/pmax | solution.py:46
  183.9 8.0 %exponential_reduce_fusion = f32[2048]{0:T(1024)S(1)} fusion(f32[2048,2048]{0,1:T(8,128)} %get-tuple-element.6, f32[2048]{0:T(1024)S(1)} %fusion.8, f32[2048]{0:T(1024)S(1)} %add_multiply_fusion.1), kind=kLoop, calls=%fused_computation.6 | loop fusion | flops 16775168 | bytes 16801792 | tf_op jit(solution)/shard_map/reduce_sum | solution.py:69
  191.9 6.6 %psum.46 = f32[2048]{0:T(1024)S(1)} all-reduce(f32[2048]{0:T(1024)S(1)} %exponential_multiply_fusion), channel_id=1, replica_groups=mesh['region'=2,'mod'=4,'obs'=4] {'obs'}, use_global_device_ids=true, to_apply=%region_21.22 | all-reduce | flops 2048 | bytes 16384 | tf_op jit(solution)/shard_map/psum | solution.py:47
  199.2 31.5 %fusion.1 = f32[2048,128]{1,0:T(8,128)} fusion(f32[2048,128]{1,0:T(8,128)S(1)} %bitcast.17, f32[2048,2048]{0,1:T(8,128)} %get-tuple-element.6, f32[2048]{0:T(1024)S(1)} %get-tuple-element.4, f32[2048]{0:T(1024)S(1)} %add_multiply_fusion.1), kind=kOutput, calls=%fused_computation.3 | convolution fusion | flops 6455033856 | bytes 18890752 | tf_op jit(solution)/shard_map/dot_general | solution.py:84
  230.7 35.3 %all-reduce.2.cloned.1.call-done = f32[2048,128]{1,0:T(8,128)} async-done(((f32[2048,128]{1,0:T(8,128)}), f32[2048,128]{1,0:T(8,128)}) %all-reduce.2.cloned.1.call-update) | async-done | bytes 1048592 | tf_op jit(solution)/shard_map/psum | solution.py:87
  (26 shorter events, 14.0 us)
Async XLA Ops:
  7.2 258.8 %all-reduce.2.cloned.1.call-start = ((), (), s32[]{:S(2)}) async-start(), calls=%async_computation | async-start | bytes 2097152 | tf_op jit(solution)/shard_map/psum | solution.py:87
  7.2 12.5 %collective-permute-start = (f32[512,128]{1,0:T(8,128)}, f32[512,128]{1,0:T(8,128)S(1)}, u32[]{:S(2)}, u32[]{:S(2)}) collective-permute-start(f32[512,128]{1,0:T(8,128)} %param.3), channel_id=1, source_target_pairs={{0,4},{4,8},{8,12},{12,0},{1,5},{5,9},{9,13},{13,1},{2,6},{6,10},{... | collective-permute-start | bytes 786440 | tf_op jit(solution)/shard_map/ppermute | solution.py:24
  10.3 13.8 %collective-permute-start.2 = (f32[512,128]{1,0:T(8,128)}, f32[512,128]{1,0:T(8,128)S(1)}, u32[]{:S(2)}, u32[]{:S(2)}) collective-permute-start(f32[512,128]{1,0:T(8,128)} %param.3), channel_id=1, source_target_pairs={{4,0},{8,4},{12,8},{0,12},{5,1},{9,5},{13,9},{1,13},{6,2},{10,6},{... | collective-permute-start | bytes 786440 | tf_op jit(solution)/shard_map/ppermute | solution.py:26
  19.8 10.4 %collective-permute-start.1 = (f32[512,128]{1,0:T(8,128)S(1)}, f32[512,128]{1,0:T(8,128)S(1)}, u32[]{:S(2)}, u32[]{:S(2)}) collective-permute-start(f32[512,128]{1,0:T(8,128)S(1)} %collective-permute-done), channel_id=1, source_target_pairs={{0,4},{4,8},{8,12},{12,0},{1,5},{5,9},{9,13},{13,1},{2,6},{6,10},{... | collective-permute-start | bytes 786440 | tf_op jit(solution)/shard_map/ppermute | solution.py:24
  170.5 28.7 %copy-start = (f32[2048]{0:T(1024)}, f32[2048]{0:T(1024)S(1)}, u32[]{:S(2)}) copy-start(f32[2048]{0:T(1024)S(1)} %add_multiply_fusion.1) | copy-start | bytes 24580
Sparse Core Ops, SparseCore 0:
  230.8 35.1 all-reduce.1
